TPU v7x, 128 devices: a whole 4x4x4 slice. The times are simulated.
128 devices in a mesh: rep: 4 (over x), fsdp: 2 (over core), tp: 16 (over z, y).
Axes of the slice: x: 4, y: 4, z: 4, core: 2. Of those that a mesh axis runs over, the one named last changes fastest.
Arguments:
- tokens: bfloat16 [8192, 2048], P(('rep', 'fsdp'), 'tp'), may hold values from -6 to 6
- cotangent: bfloat16 [8192, 2048], P(('rep', 'fsdp'), 'tp'), may hold values from -6 to 6
- frame_mask: int32 [8192], P(('rep', 'fsdp')), may hold values 0 or 1
- ln_gain: bfloat16 [2048], P('tp'), may hold values from 0.099609375 to 1.8984375
- ln_bias: bfloat16 [2048], P('tp'), may hold values from -3 to 3
- weight_in: bfloat16 [2048, 8192], P('fsdp', 'tp'), may hold values from -0.1875 to 0.1875
- weight_out: bfloat16 [8192, 2048], P('tp', 'fsdp'), may hold values from -0.09375 to 0.09375
- blocks_in: int32 [16, 64], P('fsdp', 'tp'), may hold values 0 or 1
- blocks_out: int32 [64, 16], P('tp', 'fsdp'), may hold values 0 or 1
Outputs:
- block_out: bfloat16 [8192, 2048], P(('rep', 'fsdp'), 'tp')
- input_grad: bfloat16 [8192, 2048], P(('rep', 'fsdp'), 'tp')
- grad_in: float32 [2048, 8192], P('fsdp', 'tp')
- grad_out: float32 [8192, 2048], P('tp', 'fsdp')
- grad_gain: float32 [2048], P('tp')
- grad_bias: float32 [2048], P('tp')
All inputs are finite; a program needn't handle non-finite values. No bound on the sum of `frame_mask` or of `blocks_in` or of `blocks_out` on one device may be relied on, other than what follows from the above.
Results may differ from a plain program's by a relative error of at most 0.019.
Values may be sent and summed in bfloat16 or wider, within the bound.
No kernel may reach another device: no remote copies, remote signals or barrier semaphores. Data moves between devices by JAX's collectives and lax.ppermute only.
A program may use at most 128 MiB of HBM per device.

v0:
```python
from functools import partial
import jax
import jax.numpy as jnp
from jax import lax
from jax.sharding import PartitionSpec as P

BLK = 128


def apply_blocks(weight, blocks, kind):
    row_blocks, col_blocks = blocks.shape
    shaped = weight.reshape(row_blocks, BLK, col_blocks, BLK)
    keeper = blocks.astype(kind)[:, None, :, None]
    return (shaped * keeper).reshape(weight.shape)


def contract_rows(left, right):
    return lax.dot_general(
        left, right, (((0,), (0,)), ((), ())), preferred_element_type=jnp.float32
    )


def contract_cols(left, right):
    return lax.dot_general(
        left, right, (((1,), (1,)), ((), ())), preferred_element_type=jnp.float32
    )


def on_device(
    tokens, cotangent, frame_mask, ln_gain, ln_bias, weight_in, weight_out, blocks_in, blocks_out
):
    whole_rows, whole_grad, gain_full, bias_full = (
        lax.all_gather(tokens, "tp", axis=1, tiled=True),
        lax.all_gather(cotangent, "tp", axis=1, tiled=True),
        lax.all_gather(ln_gain, "tp", axis=0, tiled=True),
        lax.all_gather(ln_bias, "tp", axis=0, tiled=True),
    )
    masked_in = apply_blocks(weight_in, blocks_in, jnp.bfloat16)
    masked_out = apply_blocks(weight_out, blocks_out, jnp.bfloat16)
    full_in, full_out = (
        lax.all_gather(masked_in, "fsdp", axis=0, tiled=True),
        lax.all_gather(masked_out, "fsdp", axis=1, tiled=True),
    )
    width = whole_rows.shape[1]
    own_width = tokens.shape[1]
    col_start = lax.axis_index("tp") * own_width
    gelu_exact = partial(jax.nn.gelu, approximate=False)
    values = whole_rows.astype(jnp.float32)
    centre = jnp.mean(values, axis=1, keepdims=True)
    centred = values - centre
    inv_std = lax.rsqrt(jnp.mean(centred * centred, axis=1, keepdims=True) + 1e-05)
    normed = centred * inv_std
    scaled = (normed * gain_full.astype(jnp.float32) + bias_full.astype(jnp.float32)).astype(
        jnp.bfloat16
    )
    hidden = jnp.dot(scaled, full_in, preferred_element_type=jnp.float32)
    active = gelu_exact(hidden).astype(jnp.bfloat16)
    partial_out = jnp.dot(active, full_out, preferred_element_type=jnp.float32)
    branch = lax.psum_scatter(
        partial_out.astype(jnp.bfloat16), "tp", scatter_dimension=1, tiled=True
    ).astype(jnp.float32)
    block_out = (tokens.astype(jnp.float32) + branch).astype(jnp.bfloat16)
    flags = frame_mask[:, None].astype(jnp.bfloat16)
    chosen = whole_grad * flags
    chosen_own = cotangent * flags
    back_active = contract_cols(chosen, full_out)
    unused, gelu_back = jax.vjp(gelu_exact, hidden)
    back_hidden = gelu_back(back_active)[0].astype(jnp.bfloat16)
    partial_normed = contract_cols(back_hidden, full_in)
    normed_own = lax.dynamic_slice_in_dim(normed, col_start, own_width, 1)
    gain_own = ln_gain.astype(jnp.float32)
    back_normed = lax.psum_scatter(
        partial_normed.astype(jnp.bfloat16), "tp", scatter_dimension=1, tiled=True
    ).astype(jnp.float32)
    back_scaled = back_normed * gain_own
    sum_plain = jnp.sum(back_scaled, axis=1)
    sum_cross = jnp.sum(back_scaled * normed_own, axis=1)
    sum_plain, sum_cross = lax.psum((sum_plain, sum_cross), "tp")
    mean_plain = (sum_plain / width)[:, None]
    mean_cross = (sum_cross / width)[:, None]
    back_rows = inv_std * (back_scaled - mean_plain - normed_own * mean_cross)
    input_grad = (chosen_own.astype(jnp.float32) + back_rows).astype(jnp.bfloat16)
    local_gain = jnp.sum(back_normed * normed_own, axis=0)
    local_bias = jnp.sum(back_normed, axis=0)
    grad_gain, grad_bias = lax.psum((local_gain, local_bias), ("rep", "fsdp"))
    term_in = contract_rows(scaled, back_hidden)
    term_out = contract_rows(active, chosen)
    shard_in, shard_out = (
        lax.psum_scatter(
            term_in.astype(jnp.bfloat16), "fsdp", scatter_dimension=0, tiled=True
        ).astype(jnp.float32),
        lax.psum_scatter(
            term_out.astype(jnp.bfloat16), "fsdp", scatter_dimension=1, tiled=True
        ).astype(jnp.float32),
    )
    shard_in, shard_out = (
        lax.psum(shard_in.astype(jnp.bfloat16), "rep").astype(jnp.float32),
        lax.psum(shard_out.astype(jnp.bfloat16), "rep").astype(jnp.float32),
    )
    grad_in = apply_blocks(shard_in, blocks_in, jnp.float32)
    grad_out = apply_blocks(shard_out, blocks_out, jnp.float32)
    return (block_out, input_grad, grad_in, grad_out, grad_gain, grad_bias)


def solution(mesh):
    placed = (
        P(("rep", "fsdp"), "tp"),
        P(("rep", "fsdp"), "tp"),
        P(("rep", "fsdp")),
        P("tp"),
        P("tp"),
        P("fsdp", "tp"),
        P("tp", "fsdp"),
        P("fsdp", "tp"),
        P("tp", "fsdp"),
    )
    return jax.shard_map(
        on_device,
        mesh=mesh,
        in_specs=placed,
        out_specs=(
            P(("rep", "fsdp"), "tp"),
            P(("rep", "fsdp"), "tp"),
            P("fsdp", "tp"),
            P("tp", "fsdp"),
            P("tp"),
            P("tp"),
        ),
        check_vma=False,
    )
```

profile of v0, /device:TPU:0, one launch (start us, length us, event | category | flops | bytes accessed | tf_op | source)
XLA Modules:
  0.0 492.1 jit_solution(3719068611543885792)
XLA Ops:
  7.2 0.0 all-gather.7.cloned.1.call-start
  7.2 0.7 all-gather.7.cloned.1.call-update
  7.9 0.0 all-gather.9.cloned.1.call-start
  7.9 0.8 fusion.34
  8.7 0.1 copy.17
  8.8 0.3 mul.149
  9.2 0.0 copy-start.2
  9.2 2.4 bitcast_multiply_fusion.3
  11.6 0.0 all-gather.9.cloned.1.call-update
  11.6 0.0 all-gather.11.cloned.1.call-start
  11.7 0.2 mul.155
  12.0 1.2 bitcast_multiply_fusion.2
  13.2 0.0 all-gather.11.cloned.1.call-update
  13.2 0.0 all-gather.13.cloned.1.call-start
  13.2 0.5 all-gather.13.cloned.1.call-update
  13.8 0.0 reduce-scatter.9.cloned.1.call-start
  13.8 22.1 %all-gather = bf16[16,1,128]{2,1,0:T(2,128)(2,1)S(1)} all-gather(bf16[1,1,128]{2,1,0:T(2,128)(2,1)S(1)} %bitcast.45), channel_id=1, replica_groups=mesh['rep'=4,'fsdp'=2,'tp'=16] {'tp'}, dimensions={0}, use_global_device_ids=true | all-gather | bytes 4352 | tf_op jit(solution)/shard_map/all_gather | solution.py:35
  36.0 19.5 %all-gather.1 = bf16[16,1,128]{2,1,0:T(2,128)(2,1)S(1)} all-gather(bf16[1,1,128]{2,1,0:T(2,128)(2,1)S(1)} %bitcast.44), channel_id=1, replica_groups=mesh['rep'=4,'fsdp'=2,'tp'=16] {'tp'}, dimensions={0}, use_global_device_ids=true | all-gather | bytes 4352 | tf_op jit(solution)/shard_map/all_gather | solution.py:36
  55.5 14.8 %all-gather.7.cloned.1.call-done = bf16[1024,2048]{1,0:T(8,128)(2,1)} async-done(((bf16[1024,128]{1,0:T(8,128)(2,1)}), bf16[1024,2048]{1,0:T(8,128)(2,1)}) %all-gather.7.cloned.1.call-update) | async-done | bytes 4194320 | tf_op jit(solution)/shard_map/all_gather | solution.py:33
  70.4 3.0 convert_reduce_fusion
  73.4 0.5 copy-done
  73.8 1.2 fusion.2
  75.1 10.1 %all-gather.9.cloned.1.call-done = bf16[2048,512]{1,0:T(8,128)(2,1)} async-done(((bf16[1024,512]{1,0:T(8,128)(2,1)}), bf16[2048,512]{1,0:T(8,128)(2,1)}) %all-gather.9.cloned.1.call-update) | async-done | bytes 2097168 | tf_op jit(solution)/shard_map/all_gather | solution.py:41
  85.1 10.5 %multiply_convert_fusion = (bf16[1024,512]{1,0:T(8,128)(2,1)S(1)}, f32[1024,512]{1,0:T(8,128)}, f32[1024,512]{1,0:T(8,128)}) fusion(bf16[2048,512]{1,0:T(8,128)(2,1)} %all-gather.9.cloned.1.call-done, f32[2048]{0:T(1024)S(1)} %bitcast.42, f32[2048]{0:T(1024)S(1)} %bitcast.40, f32[1024]{0:T(1024)S(1)} %add_rsqrt_fusion, ...), kind=kOutput, calls=%fused_computation.21 | convolution fusion | flops 2194145280 | bytes 11558912 | tf_op jit(solution)/shard_map/dot_general | solution.py:56
  95.6 5.8 %all-gather.11.cloned.1.call-done = bf16[512,2048]{1,0:T(8,128)(2,1)} async-done(((bf16[512,1024]{1,0:T(8,128)(2,1)}), bf16[512,2048]{1,0:T(8,128)(2,1)}) %all-gather.11.cloned.1.call-update) | async-done | bytes 2097168 | tf_op jit(solution)/shard_map/all_gather | solution.py:42
  101.4 61.1 %all-gather.13.cloned.1.call-done = bf16[1024,2048]{1,0:T(8,128)(2,1)} async-done(((bf16[1024,128]{1,0:T(8,128)(2,1)}), bf16[1024,2048]{1,0:T(8,128)(2,1)}) %all-gather.13.cloned.1.call-update) | async-done | bytes 4194320 | tf_op jit(solution)/shard_map/all_gather | solution.py:34
  162.5 7.1 %add_convert_fusion.1 = bf16[1024,512]{1,0:T(8,128)(2,1)S(1)} fusion(f32[1024,512]{1,0:T(8,128)} %get-tuple-element.17, f32[1024,512]{1,0:T(8,128)} %get-tuple-element.22, bf16[512,2048]{1,0:T(8,128)(2,1)} %all-gather.11.cloned.1.call-done, bf16[1024,2048]{1,0:T(8,128)(2,1)} %all-gather.13.cloned.1.call-done, bf16[1024]{0:T(1024)(128)(2,1)S(1)} %convert_element_type.88), kind=kOutput, calls=%fused_computation.18 | convolution fusion | flops 2156920832 | bytes 11536384 | tf_op jit(solution)/shard_map/dot_general | solution.py:24
  169.7 1.0 copy-done.14
  170.7 4.4 convolution_convert_fusion.2
  175.1 0.0 reduce-scatter.9.cloned.1.call-update
  175.1 0.2 reduce-scatter.11.cloned.1.call-start
  175.4 6.0 %fusion.7 = bf16[512,2048]{1,0:T(8,128)(2,1)} fusion(bf16[1024,512]{1,0:T(8,128)(2,1)S(1)} %get-tuple-element.16, bf16[1024,2048]{1,0:T(8,128)(2,1)} %all-gather.13.cloned.1.call-done, bf16[1024]{0:T(1024)(128)(2,1)S(1)} %convert_element_type.88), kind=kOutput, calls=%fused_computation.14 | convolution fusion | flops 2150629376 | bytes 7342080 | tf_op jit(solution)/shard_map/dot_general | solution.py:18
  181.3 0.0 reduce-scatter.11.cloned.1.call-update
  181.4 0.0 all-reduce.5.cloned.1.call-start
  181.4 5.3 %reduce-scatter.9.cloned.1.call-done = bf16[1024,512]{1,0:T(8,128)(2,1)} async-done(((bf16[2048,512]{1,0:T(8,128)(2,1)}), bf16[1024,512]{1,0:T(8,128)(2,1)}) %reduce-scatter.9.cloned.1.call-update) | async-done | bytes 1048592 | tf_op jit(solution)/shard_map/reduce_scatter | solution.py:89
  186.7 16.6 %reduce-scatter.11.cloned.1.call-done = bf16[512,1024]{1,0:T(8,128)(2,1)} async-done(((bf16[512,2048]{1,0:T(8,128)(2,1)}), bf16[512,1024]{1,0:T(8,128)(2,1)}) %reduce-scatter.11.cloned.1.call-update) | async-done | bytes 1048592 | tf_op jit(solution)/shard_map/reduce_scatter | solution.py:92
  203.3 0.0 all-reduce.5.cloned.1.call-update
  203.3 0.0 reduce-scatter.15.cloned.1.call-start
  203.4 5.5 %convolution_convert_fusion = bf16[1024,2048]{1,0:T(8,128)(2,1)} fusion(bf16[1024,512]{1,0:T(8,128)(2,1)} %copy-done.14, bf16[2048,512]{1,0:T(8,128)(2,1)S(1)} %copy-done.11), kind=kOutput, calls=%fused_computation.6 | convolution fusion | flops 2149580800 | bytes 7340032 | tf_op jit(solution)/shard_map/dot_general | solution.py:24
  208.9 6.4 %copy.21 = bf16[1024,2048]{0,1:T(8,128)(2,1)} copy(bf16[1024,2048]{1,0:T(8,128)(2,1)} %convolution_convert_fusion) | data formatting | bytes 8388608
  215.3 0.0 reduce-scatter.15.cloned.1.call-update
  215.3 0.0 reduce-scatter.13.cloned.1.call-start
  215.4 1.6 copy-done.12
  217.0 5.5 %convolution_convert_fusion.1 = bf16[1024,2048]{1,0:T(8,128)(2,1)} fusion(bf16[1024,512]{1,0:T(8,128)(2,1)} %copy-done.13, bf16[512,2048]{1,0:T(8,128)(2,1)S(1)} %copy-done.12), kind=kOutput, calls=%fused_computation.7 | convolution fusion | flops 2149580800 | bytes 7340032 | tf_op jit(solution)/shard_map/dot_general | solution.py:58
  222.5 6.4 %copy.19 = bf16[1024,2048]{0,1:T(8,128)(2,1)} copy(bf16[1024,2048]{1,0:T(8,128)(2,1)} %convolution_convert_fusion.1) | data formatting | bytes 8388608
  228.9 0.0 reduce-scatter.13.cloned.1.call-update
  228.9 0.1 copy.18
  229.0 6.4 %fusion = f32[1024,2048]{1,0:T(8,128)} fusion(bf16[1024,2048]{1,0:T(8,128)(2,1)} %all-gather.7.cloned.1.call-done, f32[1024]{0:T(1024)S(1)} %add_rsqrt_fusion, f32[1024]{0:T(1024)S(1)} %broadcast_multiply_fusion.2), kind=kLoop, calls=%fused_computation.2 | loop fusion | flops 6291456 | bytes 12591104 | tf_op jit(solution)/shard_map/mul | solution.py:52
  235.4 30.6 %all-reduce.5.cloned.1.call-done = (bf16[1024,512]{1,0:T(8,128)(2,1)}, bf16[512,1024]{1,0:T(8,128)(2,1)}) async-done(((bf16[1024,512]{1,0:T(8,128)(2,1)}, bf16[512,1024]{1,0:T(8,128)(2,1)}), (bf16[1024,512]{1,0:T(8,128)(2,1)}, bf16[512,1024]{1,0:T(8,128)(2,1)})) %all-reduce.5.cloned.1.call-update) | async-done | bytes 2097168 | tf_op jit(solution)/shard_map/psum | solution.py:97
  266.0 0.3 mul.177
  266.4 0.9 copy-done.4
  267.3 1.7 bitcast_multiply_fusion.1
  268.9 0.2 mul.180
  269.1 1.0 copy-done.3
  270.2 2.0 bitcast_multiply_fusion
  272.2 75.3 %reduce-scatter.15.cloned.1.call-done = bf16[128,1024]{1,0:T(8,128)(2,1)} async-done(((bf16[2048,1024]{1,0:T(8,128)(2,1)}), bf16[128,1024]{1,0:T(8,128)(2,1)}) %reduce-scatter.15.cloned.1.call-update) | async-done | bytes 262160
  347.4 1.1 copy.22
  348.5 79.2 %reduce-scatter.13.cloned.1.call-done = bf16[128,1024]{1,0:T(8,128)(2,1)} async-done(((bf16[2048,1024]{1,0:T(8,128)(2,1)}), bf16[128,1024]{1,0:T(8,128)(2,1)}) %reduce-scatter.13.cloned.1.call-update) | async-done | bytes 262160
  427.7 1.1 copy.20
  428.8 0.8 add_convert_fusion.4
  429.6 1.4 fusion.29
  431.0 13.5 %all-reduce.1 = (f32[128]{0:T(128)}, f32[128]{0:T(128)}) all-reduce(f32[128]{0:T(128)S(1)} %get-tuple-element.6, f32[128]{0:T(128)S(1)} %get-tuple-element.9), channel_id=1, replica_groups=mesh['rep'=4,'fsdp'=2,'tp'=16] {'rep','fsdp'}, use_global_device_ids=true, to_apply=%region_13.0 | all-reduce | flops 256 | bytes 2048 | tf_op jit(solution)/shard_map/psum | solution.py:85
  444.5 38.7 %all-reduce = (f32[1024]{0:T(1024)S(1)}, f32[1024]{0:T(1024)S(1)}) all-reduce(f32[1024]{0:T(1024)S(1)} %get-tuple-element.7, f32[1024]{0:T(1024)S(1)} %get-tuple-element.8), channel_id=1, replica_groups=mesh['rep'=4,'fsdp'=2,'tp'=16] {'tp'}, use_global_device_ids=true, to_apply=%region_7.0 | all-reduce | flops 2048 | bytes 16384 | tf_op jit(solution)/shard_map/psum | solution.py:78
  483.2 2.4 fusion.27
  (32 shorter events, 0.1 us)
Async XLA Ops:
  7.2 63.2 %all-gather.7.cloned.1.call-start = ((), (), s32[]{:S(2)}) async-start(), calls=%async_computation.4 | async-start | bytes 4456448 | tf_op jit(solution)/shard_map/all_gather | solution.py:33
  7.9 77.2 %all-gather.9.cloned.1.call-start = ((), (), s32[]{:S(2)}) async-start(), calls=%async_computation.5 | async-start | bytes 3145728 | tf_op jit(solution)/shard_map/all_gather | solution.py:41
  9.2 2.5 copy-start.8
  9.2 2.7 copy-start.2
  11.6 89.8 %all-gather.11.cloned.1.call-start = ((), (), s32[]{:S(2)}) async-start(), calls=%async_computation.6 | async-start | bytes 3145728 | tf_op jit(solution)/shard_map/all_gather | solution.py:42
  11.9 1.9 copy-start.10
  11.9 24.1 %copy-start.9 = (bf16[128]{0:T(256)(128)(2,1)S(1)}, bf16[128]{0:T(256)(128)(2,1)}, u32[]{:S(2)}) copy-start(bf16[128]{0:T(256)(128)(2,1)} %param.13) | copy-start | bytes 772
  11.9 43.6 %copy-start.7 = (s32[1024]{0:T(1024)S(1)}, s32[1024]{0:T(1024)}, u32[]{:S(2)}) copy-start(s32[1024]{0:T(1024)} %param.11) | copy-start | bytes 12292
  13.2 149.3 %all-gather.13.cloned.1.call-start = ((), (), s32[]{:S(2)}) async-start(), calls=%async_computation.7 | async-start | bytes 4456448 | tf_op jit(solution)/shard_map/all_gather | solution.py:34
  13.8 173.0 %reduce-scatter.9.cloned.1.call-start = ((), (), s32[]{:S(2)}) async-start(), calls=%async_computation.8 | async-start | bytes 3145728 | tf_op jit(solution)/shard_map/reduce_scatter | solution.py:89
  70.4 3.4 copy-start
  95.6 79.8 %copy-start.13 = (bf16[1024,512]{1,0:T(8,128)(2,1)}, bf16[1024,512]{1,0:T(8,128)(2,1)S(1)}, u32[]{:S(2)}) copy-start(bf16[1024,512]{1,0:T(8,128)(2,1)S(1)} %get-tuple-element.16) | copy-start | bytes 3145732
  162.5 8.1 %copy-start.1 = (bf16[1024,2048]{1,0:T(8,128)(2,1)S(1)}, bf16[1024,2048]{1,0:T(8,128)(2,1)}, u32[]{:S(2)}) copy-start(bf16[1024,2048]{1,0:T(8,128)(2,1)} %all-gather.7.cloned.1.call-done) | copy-start | bytes 12582916
  169.6 1.0 copy-start.14
  175.1 28.2 %reduce-scatter.11.cloned.1.call-start = ((), (), s32[]{:S(2)}) async-start(), calls=%async_computation.9 | async-start | bytes 3145728 | tf_op jit(solution)/shard_map/reduce_scatter | solution.py:92
  181.3 22.1 %copy-start.11 = (bf16[2048,512]{1,0:T(8,128)(2,1)S(1)}, bf16[2048,512]{1,0:T(8,128)(2,1)}, u32[]{:S(2)}) copy-start(bf16[2048,512]{1,0:T(8,128)(2,1)} %all-gather.9.cloned.1.call-done) | copy-start | bytes 6291460
  181.4 84.7 %all-reduce.5.cloned.1.call-start = ((), (), s32[]{:S(2)}) async-start(), calls=%async_computation.12 | async-start | bytes 4194304 | tf_op jit(solution)/shard_map/psum | solution.py:97
  203.3 144.1 %reduce-scatter.15.cloned.1.call-start = ((), (), s32[]{:S(2)}) async-start(), calls=%async_computation.11 | async-start | bytes 4456448
  215.3 1.6 copy-start.12
  215.3 212.4 %reduce-scatter.13.cloned.1.call-start = ((), (), s32[]{:S(2)}) async-start(), calls=%async_computation.10 | async-start | bytes 4456448
  266.0 1.2 copy-start.4
  268.9 1.2 copy-start.3
  270.2 158.7 %copy-start.5 = (bf16[1024,128]{1,0:T(8,128)(2,1)S(1)}, bf16[1024,128]{1,0:T(8,128)(2,1)}, u32[]{:S(2)}) copy-start(bf16[1024,128]{1,0:T(8,128)(2,1)} %param.9) | copy-start | bytes 786436
  272.2 211.0 %copy-start.6 = (bf16[1024,128]{1,0:T(8,128)(2,1)S(1)}, bf16[1024,128]{1,0:T(8,128)(2,1)}, u32[]{:S(2)}) copy-start(bf16[1024,128]{1,0:T(8,128)(2,1)} %param.10) | copy-start | bytes 786436
Sparse Core Ops, SparseCore 0:
  10.1 60.2 all-gather.6
  72.6 12.4 all-gather.8
  86.8 14.6 all-gather.10
  103.4 59.0 all-gather.12
  175.2 11.4 reduce-scatter.8
  189.6 13.6 reduce-scatter.10
  205.8 60.2 all-reduce.4
  269.7 77.6 reduce-scatter.14
  350.8 76.9 reduce-scatter.12
where the time goes:
time: 493 us; the launch traced here: 492 us
  waiting for transfers between devices  300 us (61%)
  blocking collectives  93.8 us (19%)
  matrix products  39 us (8%)
  other arithmetic  23.2 us (5%)
  local copies, waits for them, and re-layouts  21.3 us (4%)
  between operations  14.1 us (3%)
    unnamed x11, waiting for transfers between devices  156 us
    all_gather x1, waiting for transfers between devices, on_device(): lax.all_gather(cotangent, 'tp', axis=1, tiled=True)  61.1 us
    psum x1, blocking collectives, on_device(): sum_plain, sum_cross = lax.psum((sum_plain, sum_cross), 'tp')  38.7 us
    psum x1, waiting for transfers between devices, on_device(): lax.psum(shard_in.astype(jnp.bfloat16), 'rep').astype(jnp.float32)  30.6 us
    all_gather x1, blocking collectives, on_device(): lax.all_gather(ln_gain, 'tp', axis=0, tiled=True)  22.1 us
    unnamed x34, local copies, waits for them, and re-layouts  20 us
    all_gather x1, blocking collectives, on_device(): lax.all_gather(ln_bias, 'tp', axis=0, tiled=True)  19.5 us
    reduce_scatter x1, waiting for transfers between devices, on_device(): lax.psum_scatter(term_out.astype(jnp.bfloat16), 'fsdp', scatter_dimension...  16.6 us
  transfers between devices with their start and end apart: 9, of which 9 were waited for; matrix products, arithmetic and copies ran while one was open for 12% of the time, Pallas kernels for 0%

commit v1 on v0

--- a/solution.py
+++ b/solution.py
@@ -82,7 +82,7 @@
     input_grad = (chosen_own.astype(jnp.float32) + back_rows).astype(jnp.bfloat16)
     local_gain = jnp.sum(back_normed * normed_own, axis=0)
     local_bias = jnp.sum(back_normed, axis=0)
-    grad_gain, grad_bias = lax.psum((local_gain, local_bias), ("rep", "fsdp"))
+    grad_gain, grad_bias = lax.psum(lax.psum((local_gain, local_bias), "rep"), "fsdp")
     term_in = contract_rows(scaled, back_hidden)
     term_out = contract_rows(active, chosen)
     shard_in, shard_out = (

time: 493 us -> 493 us (level)
    psum x1 -> x2, blocking collectives: 13.5 us -> 13.4 us  [the longest x1 10.4 us: on_device(): lax.psum((local_gain, local_bias), 'rep')]
where the time goes in v1:
time: 493 us; the launch traced here: 492 us
  waiting for transfers between devices  300 us (61%)
  blocking collectives  93.8 us (19%)
  matrix products  39 us (8%)
  other arithmetic  23.2 us (5%)
  local copies, waits for them, and re-layouts  21.3 us (4%)
  between operations  14.1 us (3%)
    unnamed x11, waiting for transfers between devices  156 us
    all_gather x1, waiting for transfers between devices, on_device(): lax.all_gather(cotangent, 'tp', axis=1, tiled=True)  61.1 us
    psum x1, blocking collectives, on_device(): sum_plain, sum_cross = lax.psum((sum_plain, sum_cross), 'tp')  38.7 us
    psum x1, waiting for transfers between devices, on_device(): lax.psum(shard_in.astype(jnp.bfloat16), 'rep').astype(jnp.float32)  30.6 us
    all_gather x1, blocking collectives, on_device(): lax.all_gather(ln_gain, 'tp', axis=0, tiled=True)  22.1 us
    unnamed x34, local copies, waits for them, and re-layouts  20 us
    all_gather x1, blocking collectives, on_device(): lax.all_gather(ln_bias, 'tp', axis=0, tiled=True)  19.5 us
    reduce_scatter x1, waiting for transfers between devices, on_device(): lax.psum_scatter(term_out.astype(jnp.bfloat16), 'fsdp', scatter_dimension...  16.6 us
  transfers between devices with their start and end apart: 9, of which 9 were waited for; matrix products, arithmetic and copies ran while one was open for 12% of the time, Pallas kernels for 0%

profile of v1, /device:TPU:0, one launch (start us, length us, event | category | flops | bytes accessed | tf_op | source)
XLA Modules:
  0.0 492.1 jit_solution(1459919132903715678)
XLA Ops:
  7.2 0.0 all-gather.7.cloned.1.call-start
  7.2 0.7 all-gather.7.cloned.1.call-update
  7.9 0.0 all-gather.9.cloned.1.call-start
  7.9 0.8 fusion.34
  8.7 0.1 copy.17
  8.8 0.3 mul.149
  9.2 2.4 bitcast_multiply_fusion.3
  11.6 0.0 all-gather.9.cloned.1.call-update
  11.6 0.0 all-gather.11.cloned.1.call-start
  11.7 0.2 mul.155
  12.0 1.2 bitcast_multiply_fusion.2
  13.1 0.0 all-gather.11.cloned.1.call-update
  13.2 0.0 all-gather.13.cloned.1.call-start
  13.2 0.5 all-gather.13.cloned.1.call-update
  13.8 0.0 reduce-scatter.9.cloned.1.call-start
  13.8 22.1 %all-gather = bf16[16,1,128]{2,1,0:T(2,128)(2,1)S(1)} all-gather(bf16[1,1,128]{2,1,0:T(2,128)(2,1)S(1)} %bitcast.45), channel_id=1, replica_groups=mesh['rep'=4,'fsdp'=2,'tp'=16] {'tp'}, dimensions={0}, use_global_device_ids=true | all-gather | bytes 4352 | tf_op jit(solution)/shard_map/all_gather | solution.py:35
  36.0 19.5 %all-gather.1 = bf16[16,1,128]{2,1,0:T(2,128)(2,1)S(1)} all-gather(bf16[1,1,128]{2,1,0:T(2,128)(2,1)S(1)} %bitcast.44), channel_id=1, replica_groups=mesh['rep'=4,'fsdp'=2,'tp'=16] {'tp'}, dimensions={0}, use_global_device_ids=true | all-gather | bytes 4352 | tf_op jit(solution)/shard_map/all_gather | solution.py:36
  55.5 14.8 %all-gather.7.cloned.1.call-done = bf16[1024,2048]{1,0:T(8,128)(2,1)} async-done(((bf16[1024,128]{1,0:T(8,128)(2,1)}), bf16[1024,2048]{1,0:T(8,128)(2,1)}) %all-gather.7.cloned.1.call-update) | async-done | bytes 4194320 | tf_op jit(solution)/shard_map/all_gather | solution.py:33
  70.4 3.0 convert_reduce_fusion
  73.4 0.5 copy-done
  73.8 1.2 fusion.2
  75.1 10.1 %all-gather.9.cloned.1.call-done = bf16[2048,512]{1,0:T(8,128)(2,1)} async-done(((bf16[1024,512]{1,0:T(8,128)(2,1)}), bf16[2048,512]{1,0:T(8,128)(2,1)}) %all-gather.9.cloned.1.call-update) | async-done | bytes 2097168 | tf_op jit(solution)/shard_map/all_gather | solution.py:41
  85.1 10.5 %multiply_convert_fusion = (bf16[1024,512]{1,0:T(8,128)(2,1)S(1)}, f32[1024,512]{1,0:T(8,128)}, f32[1024,512]{1,0:T(8,128)}) fusion(bf16[2048,512]{1,0:T(8,128)(2,1)} %all-gather.9.cloned.1.call-done, f32[2048]{0:T(1024)S(1)} %bitcast.42, f32[2048]{0:T(1024)S(1)} %bitcast.40, f32[1024]{0:T(1024)S(1)} %add_rsqrt_fusion, ...), kind=kOutput, calls=%fused_computation.21 | convolution fusion | flops 2194145280 | bytes 11558912 | tf_op jit(solution)/shard_map/dot_general | solution.py:56
  95.6 5.8 %all-gather.11.cloned.1.call-done = bf16[512,2048]{1,0:T(8,128)(2,1)} async-done(((bf16[512,1024]{1,0:T(8,128)(2,1)}), bf16[512,2048]{1,0:T(8,128)(2,1)}) %all-gather.11.cloned.1.call-update) | async-done | bytes 2097168 | tf_op jit(solution)/shard_map/all_gather | solution.py:42
  101.4 61.1 %all-gather.13.cloned.1.call-done = bf16[1024,2048]{1,0:T(8,128)(2,1)} async-done(((bf16[1024,128]{1,0:T(8,128)(2,1)}), bf16[1024,2048]{1,0:T(8,128)(2,1)}) %all-gather.13.cloned.1.call-update) | async-done | bytes 4194320 | tf_op jit(solution)/shard_map/all_gather | solution.py:34
  162.5 7.1 %add_convert_fusion.1 = bf16[1024,512]{1,0:T(8,128)(2,1)S(1)} fusion(f32[1024,512]{1,0:T(8,128)} %get-tuple-element.19, f32[1024,512]{1,0:T(8,128)} %get-tuple-element.24, bf16[512,2048]{1,0:T(8,128)(2,1)} %all-gather.11.cloned.1.call-done, bf16[1024,2048]{1,0:T(8,128)(2,1)} %all-gather.13.cloned.1.call-done, bf16[1024]{0:T(1024)(128)(2,1)S(1)} %convert_element_type.88), kind=kOutput, calls=%fused_computation.18 | convolution fusion | flops 2156920832 | bytes 11536384 | tf_op jit(solution)/shard_map/dot_general | solution.py:24
  169.7 1.0 copy-done.14
  170.7 4.4 convolution_convert_fusion.2
  175.1 0.0 reduce-scatter.9.cloned.1.call-update
  175.1 0.2 reduce-scatter.11.cloned.1.call-start
  175.4 6.0 %fusion.7 = bf16[512,2048]{1,0:T(8,128)(2,1)} fusion(bf16[1024,512]{1,0:T(8,128)(2,1)S(1)} %get-tuple-element.18, bf16[1024,2048]{1,0:T(8,128)(2,1)} %all-gather.13.cloned.1.call-done, bf16[1024]{0:T(1024)(128)(2,1)S(1)} %convert_element_type.88), kind=kOutput, calls=%fused_computation.14 | convolution fusion | flops 2150629376 | bytes 7342080 | tf_op jit(solution)/shard_map/dot_general | solution.py:18
  181.4 0.0 reduce-scatter.11.cloned.1.call-update
  181.4 0.0 all-reduce.6.cloned.1.call-start
  181.4 5.3 %reduce-scatter.9.cloned.1.call-done = bf16[1024,512]{1,0:T(8,128)(2,1)} async-done(((bf16[2048,512]{1,0:T(8,128)(2,1)}), bf16[1024,512]{1,0:T(8,128)(2,1)}) %reduce-scatter.9.cloned.1.call-update) | async-done | bytes 1048592 | tf_op jit(solution)/shard_map/reduce_scatter | solution.py:89
  186.7 16.6 %reduce-scatter.11.cloned.1.call-done = bf16[512,1024]{1,0:T(8,128)(2,1)} async-done(((bf16[512,2048]{1,0:T(8,128)(2,1)}), bf16[512,1024]{1,0:T(8,128)(2,1)}) %reduce-scatter.11.cloned.1.call-update) | async-done | bytes 1048592 | tf_op jit(solution)/shard_map/reduce_scatter | solution.py:92
  203.3 0.0 all-reduce.6.cloned.1.call-update
  203.4 0.0 reduce-scatter.15.cloned.1.call-start
  203.4 5.5 %convolution_convert_fusion = bf16[1024,2048]{1,0:T(8,128)(2,1)} fusion(bf16[1024,512]{1,0:T(8,128)(2,1)} %copy-done.14, bf16[2048,512]{1,0:T(8,128)(2,1)S(1)} %copy-done.11), kind=kOutput, calls=%fused_computation.6 | convolution fusion | flops 2149580800 | bytes 7340032 | tf_op jit(solution)/shard_map/dot_general | solution.py:24
  209.0 6.4 %copy.21 = bf16[1024,2048]{0,1:T(8,128)(2,1)} copy(bf16[1024,2048]{1,0:T(8,128)(2,1)} %convolution_convert_fusion) | data formatting | bytes 8388608
  215.3 0.0 reduce-scatter.15.cloned.1.call-update
  215.4 0.0 reduce-scatter.13.cloned.1.call-start
  215.4 1.6 copy-done.12
  217.0 5.5 %convolution_convert_fusion.1 = bf16[1024,2048]{1,0:T(8,128)(2,1)} fusion(bf16[1024,512]{1,0:T(8,128)(2,1)} %copy-done.13, bf16[512,2048]{1,0:T(8,128)(2,1)S(1)} %copy-done.12), kind=kOutput, calls=%fused_computation.7 | convolution fusion | flops 2149580800 | bytes 7340032 | tf_op jit(solution)/shard_map/dot_general | solution.py:58
  222.5 6.4 %copy.19 = bf16[1024,2048]{0,1:T(8,128)(2,1)} copy(bf16[1024,2048]{1,0:T(8,128)(2,1)} %convolution_convert_fusion.1) | data formatting | bytes 8388608
  228.9 0.0 reduce-scatter.13.cloned.1.call-update
  229.0 0.1 copy.18
  229.0 6.4 %fusion = f32[1024,2048]{1,0:T(8,128)} fusion(bf16[1024,2048]{1,0:T(8,128)(2,1)} %all-gather.7.cloned.1.call-done, f32[1024]{0:T(1024)S(1)} %add_rsqrt_fusion, f32[1024]{0:T(1024)S(1)} %broadcast_multiply_fusion.2), kind=kLoop, calls=%fused_computation.2 | loop fusion | flops 6291456 | bytes 12591104 | tf_op jit(solution)/shard_map/mul | solution.py:52
  235.4 30.6 %all-reduce.6.cloned.1.call-done = (bf16[1024,512]{1,0:T(8,128)(2,1)}, bf16[512,1024]{1,0:T(8,128)(2,1)}) async-done(((bf16[1024,512]{1,0:T(8,128)(2,1)}, bf16[512,1024]{1,0:T(8,128)(2,1)}), (bf16[1024,512]{1,0:T(8,128)(2,1)}, bf16[512,1024]{1,0:T(8,128)(2,1)})) %all-reduce.6.cloned.1.call-update) | async-done | bytes 2097168 | tf_op jit(solution)/shard_map/psum | solution.py:97
  266.0 0.3 mul.177
  266.4 0.9 copy-done.4
  267.3 1.7 bitcast_multiply_fusion.1
  269.0 0.2 mul.180
  269.2 1.0 copy-done.3
  270.2 2.0 bitcast_multiply_fusion
  272.2 75.3 %reduce-scatter.15.cloned.1.call-done = bf16[128,1024]{1,0:T(8,128)(2,1)} async-done(((bf16[2048,1024]{1,0:T(8,128)(2,1)}), bf16[128,1024]{1,0:T(8,128)(2,1)}) %reduce-scatter.15.cloned.1.call-update) | async-done | bytes 262160
  347.4 1.1 copy.22
  348.6 79.2 %reduce-scatter.13.cloned.1.call-done = bf16[128,1024]{1,0:T(8,128)(2,1)} async-done(((bf16[2048,1024]{1,0:T(8,128)(2,1)}), bf16[128,1024]{1,0:T(8,128)(2,1)}) %reduce-scatter.13.cloned.1.call-update) | async-done | bytes 262160
  427.7 1.1 copy.20
  428.9 0.8 add_convert_fusion.4
  429.6 1.4 fusion.29
  431.0 10.4 %all-reduce.1 = (f32[128]{0:T(128)S(1)}, f32[128]{0:T(128)S(1)}) all-reduce(f32[128]{0:T(128)S(1)} %get-tuple-element.6, f32[128]{0:T(128)S(1)} %get-tuple-element.9), channel_id=1, replica_groups=mesh['rep'=4,'fsdp'=2,'tp'=16] {'rep'}, use_global_device_ids=true, to_apply=%region_13.0 | all-reduce | flops 256 | bytes 2048 | tf_op jit(solution)/shard_map/psum | solution.py:85
  441.5 3.0 all-reduce.2
  444.4 38.7 %all-reduce = (f32[1024]{0:T(1024)S(1)}, f32[1024]{0:T(1024)S(1)}) all-reduce(f32[1024]{0:T(1024)S(1)} %get-tuple-element.7, f32[1024]{0:T(1024)S(1)} %get-tuple-element.8), channel_id=1, replica_groups=mesh['rep'=4,'fsdp'=2,'tp'=16] {'tp'}, use_global_device_ids=true, to_apply=%region_7.0 | all-reduce | flops 2048 | bytes 16384 | tf_op jit(solution)/shard_map/psum | solution.py:78
  483.2 2.4 fusion.27
  (33 shorter events, 0.1 us)
Async XLA Ops:
  7.2 63.2 %all-gather.7.cloned.1.call-start = ((), (), s32[]{:S(2)}) async-start(), calls=%async_computation.4 | async-start | bytes 4456448 | tf_op jit(solution)/shard_map/all_gather | solution.py:33
  7.9 77.2 %all-gather.9.cloned.1.call-start = ((), (), s32[]{:S(2)}) async-start(), calls=%async_computation.5 | async-start | bytes 3145728 | tf_op jit(solution)/shard_map/all_gather | solution.py:41
  9.2 2.5 copy-start.8
  9.2 2.7 copy-start.2
  11.6 89.8 %all-gather.11.cloned.1.call-start = ((), (), s32[]{:S(2)}) async-start(), calls=%async_computation.6 | async-start | bytes 3145728 | tf_op jit(solution)/shard_map/all_gather | solution.py:42
  11.9 1.9 copy-start.10
  11.9 24.0 %copy-start.9 = (bf16[128]{0:T(256)(128)(2,1)S(1)}, bf16[128]{0:T(256)(128)(2,1)}, u32[]{:S(2)}) copy-start(bf16[128]{0:T(256)(128)(2,1)} %param.13) | copy-start | bytes 772
  11.9 43.6 %copy-start.7 = (s32[1024]{0:T(1024)S(1)}, s32[1024]{0:T(1024)}, u32[]{:S(2)}) copy-start(s32[1024]{0:T(1024)} %param.11) | copy-start | bytes 12292
  13.2 149.4 %all-gather.13.cloned.1.call-start = ((), (), s32[]{:S(2)}) async-start(), calls=%async_computation.7 | async-start | bytes 4456448 | tf_op jit(solution)/shard_map/all_gather | solution.py:34
  13.8 173.0 %reduce-scatter.9.cloned.1.call-start = ((), (), s32[]{:S(2)}) async-start(), calls=%async_computation.8 | async-start | bytes 3145728 | tf_op jit(solution)/shard_map/reduce_scatter | solution.py:89
  70.4 3.4 copy-start
  95.6 79.8 %copy-start.13 = (bf16[1024,512]{1,0:T(8,128)(2,1)}, bf16[1024,512]{1,0:T(8,128)(2,1)S(1)}, u32[]{:S(2)}) copy-start(bf16[1024,512]{1,0:T(8,128)(2,1)S(1)} %get-tuple-element.18) | copy-start | bytes 3145732
  162.5 8.1 %copy-start.1 = (bf16[1024,2048]{1,0:T(8,128)(2,1)S(1)}, bf16[1024,2048]{1,0:T(8,128)(2,1)}, u32[]{:S(2)}) copy-start(bf16[1024,2048]{1,0:T(8,128)(2,1)} %all-gather.7.cloned.1.call-done) | copy-start | bytes 12582916
  169.6 1.0 copy-start.14
  175.1 28.2 %reduce-scatter.11.cloned.1.call-start = ((), (), s32[]{:S(2)}) async-start(), calls=%async_computation.9 | async-start | bytes 3145728 | tf_op jit(solution)/shard_map/reduce_scatter | solution.py:92
  181.4 22.1 %copy-start.11 = (bf16[2048,512]{1,0:T(8,128)(2,1)S(1)}, bf16[2048,512]{1,0:T(8,128)(2,1)}, u32[]{:S(2)}) copy-start(bf16[2048,512]{1,0:T(8,128)(2,1)} %all-gather.9.cloned.1.call-done) | copy-start | bytes 6291460
  181.4 84.7 %all-reduce.6.cloned.1.call-start = ((), (), s32[]{:S(2)}) async-start(), calls=%async_computation.12 | async-start | bytes 4194304 | tf_op jit(solution)/shard_map/psum | solution.py:97
  203.4 144.1 %reduce-scatter.15.cloned.1.call-start = ((), (), s32[]{:S(2)}) async-start(), calls=%async_computation.11 | async-start | bytes 4456448
  215.3 1.6 copy-start.12
  215.4 212.4 %reduce-scatter.13.cloned.1.call-start = ((), (), s32[]{:S(2)}) async-start(), calls=%async_computation.10 | async-start | bytes 4456448
  266.0 1.2 copy-start.4
  269.0 1.2 copy-start.3
  270.2 158.7 %copy-start.5 = (bf16[1024,128]{1,0:T(8,128)(2,1)S(1)}, bf16[1024,128]{1,0:T(8,128)(2,1)}, u32[]{:S(2)}) copy-start(bf16[1024,128]{1,0:T(8,128)(2,1)} %param.9) | copy-start | bytes 786436
  272.2 211.0 %copy-start.6 = (bf16[1024,128]{1,0:T(8,128)(2,1)S(1)}, bf16[1024,128]{1,0:T(8,128)(2,1)}, u32[]{:S(2)}) copy-start(bf16[1024,128]{1,0:T(8,128)(2,1)} %param.10) | copy-start | bytes 786436
Sparse Core Ops, SparseCore 0:
  10.1 60.2 all-gather.6
  72.6 12.4 all-gather.8
  86.8 14.6 all-gather.10
  103.4 59.0 all-gather.12
  175.3 11.4 reduce-scatter.8
  189.6 13.6 reduce-scatter.10
  205.8 60.2 all-reduce.5
  269.7 77.6 reduce-scatter.14
  350.8 76.9 reduce-scatter.12
